TPU v7x, 256 devices: a whole 4x4x8 slice. The times are simulated.
256 devices in a mesh: dp: 16 (over y_lo, z), fsdp: 16 (over x, y_hi, core).
Axes of the slice: x: 4, y: 4 (y_hi: 2, y_lo: 2; y = y_hi * 2 + y_lo), z: 8, core: 2. Of those that a mesh axis runs over, the one named last changes fastest.
Arguments:
- latents: bfloat16 [1024, 8, 8, 640], P(('dp', 'fsdp'))
- bucket: int32 [1024], P(('dp', 'fsdp')), may hold values from 0 to 39
- cotangent: bfloat16 [1024, 4, 4, 640], P(('dp', 'fsdp')), may hold values from -6 to 6
- tile_count: int32 [256], P(('dp', 'fsdp')), may hold values from 1 to 4, as said below
- cond_table: float32 [40, 640], replicated, may hold values from -3 to 3
- norm_gain: float32 [640], replicated, may hold values from 0.1 to 1.9
- norm_shift: float32 [640], replicated, may hold values from -3 to 3
- conv_bias: float32 [640], replicated, may hold values from -3 to 3
- down_bias: float32 [640], replicated, may hold values from -3 to 3
- conv_weight: bfloat16 [5760, 640], P('fsdp'), may hold values from -0.078125 to 0.078125
- down_weight: bfloat16 [5760, 640], P('fsdp'), may hold values from -0.078125 to 0.078125
Outputs:
- block_output: bfloat16 [1024, 4, 4, 640], P(('dp', 'fsdp'))
- grad_input: bfloat16 [1024, 8, 8, 640], P(('dp', 'fsdp'))
- grad_conv: float32 [5760, 640], P('fsdp')
- grad_affine: float32 [3, 640], replicated
Inputs may be any that keep to these rules, and one draw needn't show every extreme that they name: Slots 0 to tile_count - 1 of a device are live; some device holds exactly 4 live tiles.
All inputs are finite; a program needn't handle non-finite values.
Results may differ from a plain program's by a relative error of at most 0.005.
Values may be sent and summed in bfloat16 or wider, within the bound.
No kernel may reach another device: no remote copies, remote signals or barrier semaphores. Data moves between devices by JAX's collectives and lax.ppermute only.
A program may use at most 128 MiB of HBM per device.

v0:
```python
import math
import jax
import jax.numpy as jnp
from jax import lax
from jax.sharding import PartitionSpec as P

GROUPS = 32
CONV_DIMS = ("NHWC", "HWIO", "NHWC")
BACK_DIMS = ("NHWC", "HWOI", "NHWC")


def group_mean(channel_sums, per_group):
    tiles, channels = channel_sums.shape
    width = channels // GROUPS
    grouped = channel_sums.reshape(tiles, GROUPS, width).sum(axis=-1) / per_group
    return jnp.repeat(grouped, width, axis=1)


def shifted(padded, tap, tile_side):
    row_off = tap // 3
    col_off = tap % 3
    return lax.dynamic_slice(
        padded, (0, row_off, col_off, 0), (padded.shape[0], tile_side, tile_side, padded.shape[3])
    )


def body(
    latents,
    bucket,
    cotangent,
    tile_count,
    cond_table,
    norm_gain,
    norm_shift,
    conv_bias,
    down_bias,
    conv_weight,
    down_weight,
):
    slot_total, tile_side, _, channels = latents.shape
    row_block = conv_weight.shape[0]
    conv_full = lax.all_gather(conv_weight, "fsdp", axis=0, tiled=True)
    down_full = lax.all_gather(down_weight, "fsdp", axis=0, tiled=True)
    conv_kernel = conv_full.reshape(3, 3, channels, channels)
    down_kernel = down_full.reshape(3, 3, channels, channels)
    live = jnp.arange(slot_total, dtype=jnp.int32) < tile_count[0]
    live4 = live[:, None, None, None]
    masked_cot = jnp.where(live4, cotangent, jnp.zeros_like(cotangent))
    per_group = tile_side * tile_side * (channels // GROUPS)
    values = latents.astype(jnp.float32)
    center = group_mean(jnp.sum(values, axis=(1, 2)), per_group)
    deviation = values - center[:, None, None, :]
    spread = group_mean(jnp.sum(deviation * deviation, axis=(1, 2)), per_group)
    inv_std = lax.rsqrt(spread + 1e-05)[:, None, None, :]
    normed = deviation * inv_std
    pre_act = normed * norm_gain + norm_shift
    sigmoid_v = jax.nn.sigmoid(pre_act)
    activated = (pre_act * sigmoid_v).astype(jnp.bfloat16)
    act_all = lax.all_gather(activated, "fsdp", axis=0, tiled=True)
    conditioning = cond_table[bucket]
    conv_out = lax.conv_general_dilated(
        activated,
        conv_kernel,
        (1, 1),
        ((1, 1), (1, 1)),
        dimension_numbers=CONV_DIMS,
        preferred_element_type=jnp.float32,
    )
    conv_out = conv_out + conv_bias + conditioning[:, None, None, :]
    residual = (values + conv_out).astype(jnp.bfloat16)
    down_out = lax.conv_general_dilated(
        residual,
        down_kernel,
        (2, 2),
        ((1, 1), (1, 1)),
        dimension_numbers=CONV_DIMS,
        preferred_element_type=jnp.float32,
    )
    block_output = (down_out + down_bias).astype(jnp.bfloat16)
    block_output = jnp.where(live4, block_output, jnp.zeros_like(block_output))
    grad_resid = lax.conv_general_dilated(
        masked_cot,
        down_kernel[::-1, ::-1],
        (1, 1),
        ((1, 2), (1, 2)),
        lhs_dilation=(2, 2),
        dimension_numbers=BACK_DIMS,
        preferred_element_type=jnp.float32,
    )
    grad_hidden = grad_resid.astype(jnp.bfloat16)
    grad_act = lax.conv_general_dilated(
        grad_hidden,
        conv_kernel[::-1, ::-1],
        (1, 1),
        ((1, 1), (1, 1)),
        dimension_numbers=BACK_DIMS,
        preferred_element_type=jnp.float32,
    )
    grad_pre = grad_act * sigmoid_v * (1.0 + pre_act * (1.0 - sigmoid_v))
    scaled = grad_pre * norm_gain
    mean_one = group_mean(jnp.sum(scaled, axis=(1, 2)), per_group)[:, None, None, :]
    mean_two = group_mean(jnp.sum(scaled * normed, axis=(1, 2)), per_group)[:, None, None, :]
    grad_input = (grad_resid + inv_std * (scaled - mean_one - normed * mean_two)).astype(
        jnp.bfloat16
    )
    affine = jnp.stack(
        [
            jnp.sum(grad_pre * normed, axis=(0, 1, 2)),
            jnp.sum(grad_pre, axis=(0, 1, 2)),
            jnp.sum(grad_resid, axis=(0, 1, 2)),
        ]
    )
    affine_hi = affine.astype(jnp.bfloat16)
    affine_lo = (affine - affine_hi.astype(jnp.float32)).astype(jnp.bfloat16)
    hid_rows = grad_hidden.reshape(-1, channels)
    sent = jnp.concatenate([hid_rows, affine_hi, affine_lo], axis=0)
    sent_all = lax.all_gather(sent, "fsdp", axis=0, tiled=False)
    hid_all = sent_all[:, : hid_rows.shape[0]].reshape(-1, channels)
    affine_parts = sent_all[:, hid_rows.shape[0] :].astype(jnp.float32)
    affine_fsdp = jnp.sum(affine_parts[:, :3] + affine_parts[:, 3:], axis=0)
    first_row = lax.axis_index("fsdp") * row_block
    first_tap = first_row // channels
    first_chan = first_row % channels
    span = (row_block + channels - 1) // channels + 1
    act_pad = jnp.pad(act_all, ((0, 0), (1, 1), (1, 1), (0, 0)))
    taps = [shifted(act_pad, jnp.minimum(first_tap + extra, 8), tile_side) for extra in range(span)]
    tap_cols = jnp.concatenate(taps, axis=-1)
    own_cols = lax.dynamic_slice_in_dim(tap_cols, first_chan, row_block, axis=3)
    weight_term = lax.dot_general(
        own_cols.reshape(-1, row_block),
        hid_all,
        (((0,), (0,)), ((), ())),
        preferred_element_type=jnp.float32,
    )
    loss_scale = 4.0 / math.sqrt(
        tile_side * tile_side * slot_total * lax.axis_size("dp") * lax.axis_size("fsdp")
    )
    summed = lax.psum(jnp.concatenate([weight_term, affine_fsdp], axis=0) * loss_scale, "dp")
    grad_conv = summed[:row_block]
    grad_affine = summed[row_block:]
    return (block_output, grad_input, grad_conv, grad_affine)


def solution(mesh):
    placed = (
        P(("dp", "fsdp"), None, None, None),
        P(("dp", "fsdp")),
        P(("dp", "fsdp"), None, None, None),
        P(("dp", "fsdp")),
        P(),
        P(),
        P(),
        P(),
        P(),
        P("fsdp", None),
        P("fsdp", None),
    )
    return jax.shard_map(
        body,
        mesh=mesh,
        in_specs=placed,
        out_specs=(
            P(("dp", "fsdp"), None, None, None),
            P(("dp", "fsdp"), None, None, None),
            P("fsdp", None),
            P(),
        ),
        check_vma=False,
    )
```

profile of v0, /device:TPU:2, one launch (start us, length us, event | category | flops | bytes accessed | tf_op | source)
XLA Modules:
  0.0 456.9 jit_solution(273286597701240359)
XLA Ops:
  7.3 0.7 all-gather.9.cloned.1.call-update
  8.0 0.7 all-gather.7.cloned.1.call-update
  9.4 1.2 convert_reduce_fusion
  10.9 0.1 sub.39
  11.0 1.3 fusion.20
  12.6 0.1 rsqrt.12
  12.8 73.6 %all-gather.9.cloned.1.call-done = bf16[5760,640]{1,0:T(8,128)(2,1)} async-done(((bf16[360,640]{1,0:T(8,128)(2,1)}), bf16[5760,640]{1,0:T(8,128)(2,1)}) %all-gather.9.cloned.1.call-update) | async-done | bytes 7372816 | tf_op jit(solution)/shard_map/all_gather | solution.py:43
  86.4 5.5 %fusion.28 = (bf16[4,8,8,640]{3,0,2,1:T(4,128)(2,1)S(1)}, f32[4,8,8,640]{3,0,2,1:T(4,128)S(1)}) fusion(bf16[3,3,640,640]{3,2,1,0:T(8,128)(2,1)} %bitcast.23, bf16[4,4,4,640]{3,2,1,0:T(4,128)(2,1)} %param.13, pred[4]{0:T(512)(128)(4,1)S(1)} %iota_compare_fusion), kind=kOutput, calls=%fused_computation.55 | convolution fusion | flops 396697600 | bytes 8437764 | tf_op jit(solution)/shard_map/conv_general_dilated | solution.py:81
  91.8 69.0 %all-gather.7.cloned.1.call-done = bf16[5760,640]{1,0:T(8,128)(2,1)} async-done(((bf16[360,640]{1,0:T(8,128)(2,1)}), bf16[5760,640]{1,0:T(8,128)(2,1)}) %all-gather.7.cloned.1.call-update) | async-done | bytes 7372816 | tf_op jit(solution)/shard_map/all_gather | solution.py:42
  160.8 7.6 %fusion.19 = (f32[640]{0:T(1024)S(1)}, f32[4,640]{1,0:T(4,128)S(1)}, f32[4,640]{1,0:T(4,128)S(1)}, f32[640]{0:T(1024)S(1)}, f32[4,8,8,640]{3,0,2,1:T(4,128)S(1)}) fusion(f32[4,640]{1,0:T(4,128)S(1)} %rsqrt.12, f32[4,640]{1,0:T(4,128)S(1)} %sub.39, bf16[4,8,8,640]{3,2,1,0:T(8,128)(2,1)S(1)} %copy-done.1, f32[640]{0:T(1024)S(1)} %copy-done.4, ...), kind=kOutput, calls=%fused_computation.30 | convolution fusion | flops 1589241600 | bytes 8734720 | tf_op jit(solution)/shard_map/conv_general_dilated | solution.py:91
  168.7 0.1 mul.79
  168.9 0.1 reshape.61
  169.2 0.1 sub.43
  169.3 1.6 fusion.27
  170.9 0.8 copy.27
  171.9 0.8 maximum_bitcast_fusion
  172.7 0.2 all-reduce.3.cloned.1.call-start
  173.1 0.6 gather_fusion
  173.7 62.0 %all-gather.11.cloned.1.call-done = bf16[64,8,8,640]{3,2,1,0:T(8,128)(2,1)} async-done(((bf16[4,8,8,640]{3,2,1,0:T(8,128)(2,1)}), bf16[64,8,8,640]{3,2,1,0:T(8,128)(2,1)}) %all-gather.11.cloned.1.call-update) | async-done | bytes 5242896 | tf_op jit(solution)/shard_map/all_gather | solution.py:59
  235.7 11.6 %pad_dynamic-slice_fusion = (bf16[64,8,8,640]{3,2,1,0:T(8,128)(2,1)}, bf16[64,8,8,640]{3,2,1,0:T(8,128)(2,1)}) fusion(s32[]{:T(128)S(6)} %select_n.59, s32[]{:T(128)S(6)} %select_n.61, bf16[64,8,8,640]{3,2,1,0:T(8,128)(2,1)} %all-gather.11.cloned.1.call-done, s32[]{:T(128)S(6)} %select_n.55, s32[]{:T(128)S(6)} %select_n.57), kind=kLoop, calls=%fused_computation.1 | loop fusion | bytes 15728656 | tf_op jit(solution)/shard_map/dynamic_slice | solution.py:22
  247.3 5.0 %fusion = bf16[64,8,8,360]{3,2,1,0:T(8,128)(2,1)S(1)} fusion(s32[]{:T(128)S(6)} %select_n.63, bf16[64,8,8,640]{3,2,1,0:T(8,128)(2,1)} %get-tuple-element.21, bf16[64,8,8,640]{3,2,1,0:T(8,128)(2,1)} %get-tuple-element.20), kind=kLoop, calls=%fused_computation.5 | loop fusion | flops 5898240 | bytes 13434884 | tf_op jit(solution)/shard_map/concatenate | solution.py:127
  252.3 51.1 %all-gather.13.cloned.1.call-done = bf16[16,262,640]{2,1,0:T(8,128)(2,1)} async-done(((bf16[1,262,640]{2,1,0:T(8,128)(2,1)}), bf16[16,262,640]{2,1,0:T(8,128)(2,1)}) %all-gather.13.cloned.1.call-update) | async-done | bytes 5365776 | tf_op jit(solution)/shard_map/all_gather | solution.py:117
  303.4 1.1 slice_convert_fusion
  304.5 1.4 slice-done
  305.9 2.5 fusion.29
  308.4 1.0 maximum_multiply_fusion
  309.5 12.0 %fusion.6 = bf16[4,4,4,640]{3,0,2,1:T(4,128)(2,1)S(1)} fusion(bf16[3,3,640,640]{3,2,1,0:T(8,128)(2,1)} %bitcast.24, f32[640]{0:T(1024)S(1)} %copy-done.5, pred[4]{0:T(512)(128)(4,1)S(1)} %iota_compare_fusion, bf16[3,3,640,640]{3,2,1,0:T(8,128)(2,1)} %bitcast.27, f32[4,640]{1,0:T(4,128)S(1)} %gather_fusion, f32[640]{0:T(1024)S(1)} %copy-done.6, ...), kind=kOutput, calls=%fused_computation.14 | convolution fusion | flops 1985044480 | bytes 15196164 | tf_op jit(solution)/shard_map/conv_general_dilated | solution.py:71
  321.6 0.7 copy.29
  322.2 0.8 copy.30
  323.0 123.9 %all-reduce.3.cloned.1.call-done = f32[363,640]{1,0:T(8,128)} async-done(((f32[363,640]{1,0:T(8,128)}), f32[363,640]{1,0:T(8,128)}) %all-reduce.3.cloned.1.call-update) | async-done | bytes 929296 | tf_op jit(solution)/shard_map/psum | solution.py:138
  446.8 1.3 slice.31
  448.2 2.2 slice.30
  (49 shorter events, 1.4 us)
Async XLA Ops:
  7.2 165.9 %copy-start = (f32[40,640]{1,0:T(8,128)S(1)}, f32[40,640]{1,0:T(8,128)}, u32[]{:S(2)}) copy-start(f32[40,640]{1,0:T(8,128)} %param.15) | copy-start | bytes 307204
  7.2 153.7 %copy-start.1 = (bf16[4,8,8,640]{3,2,1,0:T(8,128)(2,1)S(1)}, bf16[4,8,8,640]{3,2,1,0:T(8,128)(2,1)}, u32[]{:S(2)}) copy-start(bf16[4,8,8,640]{3,2,1,0:T(8,128)(2,1)} %param.11) | copy-start | bytes 983044
  7.2 153.6 %copy-start.3 = (f32[640]{0:T(1024)S(1)}, f32[640]{0:T(1024)}, u32[]{:S(2)}) copy-start(f32[640]{0:T(1024)} %param.17) | copy-start | bytes 7684
  7.2 153.6 %copy-start.4 = (f32[640]{0:T(1024)S(1)}, f32[640]{0:T(1024)}, u32[]{:S(2)}) copy-start(f32[640]{0:T(1024)} %param.16) | copy-start | bytes 7684
  7.2 79.1 %all-gather.9.cloned.1.call-start = ((), (), s32[]{:S(2)}) async-start(), calls=%async_computation.1 | async-start | bytes 7833600 | tf_op jit(solution)/shard_map/all_gather | solution.py:43
  7.9 152.9 %all-gather.7.cloned.1.call-start = ((), (), s32[]{:S(2)}) async-start(), calls=%async_computation | async-start | bytes 7833600 | tf_op jit(solution)/shard_map/all_gather | solution.py:42
  8.7 227.0 %all-gather.11.cloned.1.call-start = ((), (), s32[]{:S(2)}) async-start(), calls=%async_computation.2 | async-start | bytes 5570560 | tf_op jit(solution)/shard_map/all_gather | solution.py:59
  160.8 12.2 %copy-start.7 = (s32[4]{0:T(128)S(1)}, s32[4]{0:T(128)}, u32[]{:S(2)}) copy-start(s32[4]{0:T(128)} %param.12) | copy-start | bytes 52
  171.7 131.6 %all-gather.13.cloned.1.call-start = ((), (), s32[]{:S(2)}) async-start(), calls=%async_computation.4 | async-start | bytes 5744640 | tf_op jit(solution)/shard_map/all_gather | solution.py:117
  172.7 274.1 %all-reduce.3.cloned.1.call-start = ((), (), s32[]{:S(2)}) async-start(), calls=%async_computation.3 | async-start | bytes 1884160 | tf_op jit(solution)/shard_map/psum | solution.py:138
  303.3 2.6 slice-start
  305.9 3.6 copy-start.5
  305.9 3.6 copy-start.6
  309.5 12.7 %copy-start.2 = (bf16[4,8,8,640]{3,0,2,1:T(4,128)(2,1)S(1)}, bf16[4,8,8,640]{3,0,2,1:T(4,128)(2,1)}, u32[]{:S(2)}) copy-start(bf16[4,8,8,640]{3,0,2,1:T(4,128)(2,1)} %get-tuple-element.23) | copy-start | bytes 983044
Sparse Core Ops, SparseCore 0:
  10.8 75.4 all-gather.8
  89.2 71.6 all-gather.6
  171.9 63.7 all-gather.10
  238.9 64.4 all-gather.12
  309.6 137.2 all-reduce.2
where the time goes:
time: 457 us
  waiting for transfers between devices  381 us (83%)
  matrix products  27.6 us (6%)
  local copies, waits for them, and re-layouts  20.6 us (5%)
  between operations  14.8 us (3%)
  other arithmetic  12.5 us (3%)
    psum x1, waiting for transfers between devices, body(): lax.psum(jnp.concatenate([weight_term, affine_fsdp], axis=0) * loss_scale...  124 us
    all_gather x1, waiting for transfers between devices, body(): down_full = lax.all_gather(down_weight, 'fsdp', axis=0, tiled=True)  73.6 us
    all_gather x1, waiting for transfers between devices, body(): conv_full = lax.all_gather(conv_weight, 'fsdp', axis=0, tiled=True)  69 us
    all_gather x1, waiting for transfers between devices, body(): act_all = lax.all_gather(activated, 'fsdp', axis=0, tiled=True)  62 us
    all_gather x1, waiting for transfers between devices, body(): sent_all = lax.all_gather(sent, 'fsdp', axis=0, tiled=False)  51.1 us
    conv_general_dilated x1, matrix products, body(): lax.conv_general_dilated(residual, down_kernel, (2, 2), ((1, 1), (1, 1)),...  12 us
    dynamic_slice x1, local copies, waits for them, and re-layouts, shifted(): lax.dynamic_slice(padded, (0, row_off, col_off, 0), (padded.shape[0], til...  11.6 us
  transfers between devices with their start and end apart: 5, of which 5 were waited for; matrix products, arithmetic and copies ran while one was open for 9% of the time, Pallas kernels for 0%

commit v1 on v0

--- a/solution.py
+++ b/solution.py
@@ -7,6 +7,7 @@
 GROUPS = 32
 CONV_DIMS = ("NHWC", "HWIO", "NHWC")
 BACK_DIMS = ("NHWC", "HWOI", "NHWC")
+handle_series_all = lambda buf: jnp.sum(lax.all_gather(buf, axis_name="dp"), 0)
 
 
 def group_mean(channel_sums, per_group):
@@ -135,7 +136,7 @@
     loss_scale = 4.0 / math.sqrt(
         tile_side * tile_side * slot_total * lax.axis_size("dp") * lax.axis_size("fsdp")
     )
-    summed = lax.psum(jnp.concatenate([weight_term, affine_fsdp], axis=0) * loss_scale, "dp")
+    summed = handle_series_all(jnp.concatenate([weight_term, affine_fsdp], axis=0) * loss_scale)
     grad_conv = summed[:row_block]
     grad_affine = summed[row_block:]
     return (block_output, grad_input, grad_conv, grad_affine)

time: 457 us -> 492 us (1.077)
  waiting for transfers between devices: 381 us -> 411 us
  other arithmetic: 12.5 us -> 18.6 us
    all_gather x0 -> x1, waiting for transfers between devices: none -> 153 us  [lax.all_gather(buf, axis_name='dp')]
    psum x1 -> x0, waiting for transfers between devices: 124 us -> none  [body(): lax.psum(jnp.concatenate([weight_term, affine_fsdp], axis=0) * loss_scale...]
    reduce_sum x0 -> x1, other arithmetic: none -> 6.1 us  [jnp.sum(lax.all_gather(buf, axis_name='dp'), 0)]
  transfers between devices with their start and end apart: 5 -> 5, of which waited for: 5 -> 5; matrix products, arithmetic and copies ran while one was open for 9% -> 8% of each run, Pallas kernels for 0% -> 0%
where the time goes in v1:
time: 492 us; the launch traced here: 491 us
  waiting for transfers between devices  411 us (84%)
  matrix products  27.6 us (6%)
  local copies, waits for them, and re-layouts  18.7 us (4%)
  other arithmetic  18.6 us (4%)
  between operations  14.8 us (3%)
    all_gather x1, waiting for transfers between devices, lax.all_gather(buf, axis_name='dp')  153 us
    all_gather x1, waiting for transfers between devices, body(): down_full = lax.all_gather(down_weight, 'fsdp', axis=0, tiled=True)  73.6 us
    all_gather x1, waiting for transfers between devices, body(): conv_full = lax.all_gather(conv_weight, 'fsdp', axis=0, tiled=True)  69 us
    all_gather x1, waiting for transfers between devices, body(): act_all = lax.all_gather(activated, 'fsdp', axis=0, tiled=True)  62.6 us
    all_gather x1, waiting for transfers between devices, body(): sent_all = lax.all_gather(sent, 'fsdp', axis=0, tiled=False)  51.1 us
    conv_general_dilated x1, matrix products, body(): lax.conv_general_dilated(residual, down_kernel, (2, 2), ((1, 1), (1, 1)),...  12 us
    dynamic_slice x1, local copies, waits for them, and re-layouts, shifted(): lax.dynamic_slice(padded, (0, row_off, col_off, 0), (padded.shape[0], til...  11.6 us
  transfers between devices with their start and end apart: 5, of which 5 were waited for; matrix products, arithmetic and copies ran while one was open for 8% of the time, Pallas kernels for 0%

profile of v1, /device:TPU:2, one launch (start us, length us, event | category | flops | bytes accessed | tf_op | source)
XLA Modules:
  0.0 491.1 jit_solution(2496688177854236890)
XLA Ops:
  7.3 0.7 all-gather.10.cloned.1.call-update
  8.0 0.7 all-gather.8.cloned.1.call-update
  9.4 1.2 convert_reduce_fusion
  10.9 0.1 sub.39
  11.0 1.3 fusion.20
  12.6 0.1 rsqrt.12
  12.8 73.6 %all-gather.10.cloned.1.call-done = bf16[5760,640]{1,0:T(8,128)(2,1)} async-done(((bf16[360,640]{1,0:T(8,128)(2,1)}), bf16[5760,640]{1,0:T(8,128)(2,1)}) %all-gather.10.cloned.1.call-update) | async-done | bytes 7372816 | tf_op jit(solution)/shard_map/all_gather | solution.py:44
  86.4 5.5 %fusion.28 = (bf16[4,8,8,640]{3,0,2,1:T(4,128)(2,1)S(1)}, f32[4,8,8,640]{3,0,2,1:T(4,128)S(1)}) fusion(bf16[3,3,640,640]{3,2,1,0:T(8,128)(2,1)} %bitcast.26, bf16[4,4,4,640]{3,2,1,0:T(4,128)(2,1)} %param.13, pred[4]{0:T(512)(128)(4,1)S(1)} %iota_compare_fusion), kind=kOutput, calls=%fused_computation.56 | convolution fusion | flops 396697600 | bytes 8437764 | tf_op jit(solution)/shard_map/conv_general_dilated | solution.py:82
  91.8 69.0 %all-gather.8.cloned.1.call-done = bf16[5760,640]{1,0:T(8,128)(2,1)} async-done(((bf16[360,640]{1,0:T(8,128)(2,1)}), bf16[5760,640]{1,0:T(8,128)(2,1)}) %all-gather.8.cloned.1.call-update) | async-done | bytes 7372816 | tf_op jit(solution)/shard_map/all_gather | solution.py:43
  160.8 7.6 %fusion.19 = (f32[640]{0:T(1024)S(1)}, f32[4,640]{1,0:T(4,128)S(1)}, f32[4,640]{1,0:T(4,128)S(1)}, f32[640]{0:T(1024)S(1)}, f32[4,8,8,640]{3,0,2,1:T(4,128)S(1)}) fusion(f32[4,640]{1,0:T(4,128)S(1)} %rsqrt.12, f32[4,640]{1,0:T(4,128)S(1)} %sub.39, bf16[4,8,8,640]{3,2,1,0:T(8,128)(2,1)S(1)} %copy-done.1, f32[640]{0:T(1024)S(1)} %copy-done.4, ...), kind=kOutput, calls=%fused_computation.31 | convolution fusion | flops 1589241600 | bytes 8734720 | tf_op jit(solution)/shard_map/conv_general_dilated | solution.py:92
  168.7 0.1 mul.86
  169.2 0.1 sub.43
  169.3 1.6 fusion.27
  170.9 0.8 copy.27
  171.9 0.8 maximum_bitcast_fusion
  172.7 0.2 all-gather.14.cloned.1.call-start
  173.0 62.6 %all-gather.12.cloned.1.call-done = bf16[64,8,8,640]{3,2,1,0:T(8,128)(2,1)} async-done(((bf16[4,8,8,640]{3,2,1,0:T(8,128)(2,1)}), bf16[64,8,8,640]{3,2,1,0:T(8,128)(2,1)}) %all-gather.12.cloned.1.call-update) | async-done | bytes 5242896 | tf_op jit(solution)/shard_map/all_gather | solution.py:60
  235.6 11.6 %pad_dynamic-slice_fusion = (bf16[64,8,8,640]{3,2,1,0:T(8,128)(2,1)}, bf16[64,8,8,640]{3,2,1,0:T(8,128)(2,1)}) fusion(s32[]{:T(128)S(6)} %select_n.59, s32[]{:T(128)S(6)} %select_n.61, bf16[64,8,8,640]{3,2,1,0:T(8,128)(2,1)} %all-gather.12.cloned.1.call-done, s32[]{:T(128)S(6)} %select_n.55, s32[]{:T(128)S(6)} %select_n.57), kind=kLoop, calls=%fused_computation.1 | loop fusion | bytes 15728656 | tf_op jit(solution)/shard_map/dynamic_slice | solution.py:23
  247.3 5.0 %fusion = bf16[64,8,8,360]{3,2,1,0:T(8,128)(2,1)S(1)} fusion(s32[]{:T(128)S(6)} %select_n.63, bf16[64,8,8,640]{3,2,1,0:T(8,128)(2,1)} %get-tuple-element.21, bf16[64,8,8,640]{3,2,1,0:T(8,128)(2,1)} %get-tuple-element.20), kind=kLoop, calls=%fused_computation.5 | loop fusion | flops 5898240 | bytes 13434884 | tf_op jit(solution)/shard_map/concatenate | solution.py:128
  252.3 51.1 %all-gather.16.cloned.1.call-done = bf16[16,262,640]{2,1,0:T(8,128)(2,1)} async-done(((bf16[1,262,640]{2,1,0:T(8,128)(2,1)}), bf16[16,262,640]{2,1,0:T(8,128)(2,1)}) %all-gather.16.cloned.1.call-update) | async-done | bytes 5365776 | tf_op jit(solution)/shard_map/all_gather | solution.py:118
  303.3 1.1 slice_convert_fusion
  304.5 1.4 slice-done
  305.9 2.5 convolution_bitcast_fusion
  308.4 1.1 maximum_multiply_fusion
  309.6 0.6 gather_fusion
  310.2 12.0 %fusion.6 = bf16[4,4,4,640]{3,0,2,1:T(4,128)(2,1)S(1)} fusion(bf16[3,3,640,640]{3,2,1,0:T(8,128)(2,1)} %bitcast.27, f32[640]{0:T(1024)S(1)} %copy-done.5, pred[4]{0:T(512)(128)(4,1)S(1)} %iota_compare_fusion, bf16[3,3,640,640]{3,2,1,0:T(8,128)(2,1)} %bitcast.31, f32[4,640]{1,0:T(4,128)S(1)} %gather_fusion, f32[640]{0:T(1024)S(1)} %copy-done.6, ...), kind=kOutput, calls=%fused_computation.15 | convolution fusion | flops 1985044480 | bytes 15196164 | tf_op jit(solution)/shard_map/conv_general_dilated | solution.py:72
  322.2 0.7 copy.29
  322.9 0.8 copy.30
  323.6 153.2 %all-gather.14.cloned.1.call-done = f32[16,363,640]{2,1,0:T(8,128)} async-done(((f32[1,363,640]{2,1,0:T(8,128)}), f32[16,363,640]{2,1,0:T(8,128)}) %all-gather.14.cloned.1.call-update) | async-done | bytes 14868496 | tf_op jit(solution)/shard_map/all_gather | solution.py:10
  476.9 6.1 %reduce_sum.129 = f32[363,640]{1,0:T(8,128)S(1)} reduce(f32[16,363,640]{2,1,0:T(8,128)} %all-gather.14.cloned.1.call-done, f32[]{:T(128)} %constant.51.clone.1), dimensions={0}, to_apply=%region_12.13 | reduce | flops 3484800 | bytes 15797764 | tf_op jit(solution)/shard_map/reduce_sum | solution.py:10
  483.0 0.6 slice.31
  483.6 1.0 slice.30
  (50 shorter events, 1.5 us)
Async XLA Ops:
  7.2 302.4 %copy-start = (f32[40,640]{1,0:T(8,128)S(1)}, f32[40,640]{1,0:T(8,128)}, u32[]{:S(2)}) copy-start(f32[40,640]{1,0:T(8,128)} %param.15) | copy-start | bytes 307204
  7.2 153.7 %copy-start.1 = (bf16[4,8,8,640]{3,2,1,0:T(8,128)(2,1)S(1)}, bf16[4,8,8,640]{3,2,1,0:T(8,128)(2,1)}, u32[]{:S(2)}) copy-start(bf16[4,8,8,640]{3,2,1,0:T(8,128)(2,1)} %param.11) | copy-start | bytes 983044
  7.2 153.6 %copy-start.3 = (f32[640]{0:T(1024)S(1)}, f32[640]{0:T(1024)}, u32[]{:S(2)}) copy-start(f32[640]{0:T(1024)} %param.17) | copy-start | bytes 7684
  7.2 153.6 %copy-start.4 = (f32[640]{0:T(1024)S(1)}, f32[640]{0:T(1024)}, u32[]{:S(2)}) copy-start(f32[640]{0:T(1024)} %param.16) | copy-start | bytes 7684
  7.2 79.1 %all-gather.10.cloned.1.call-start = ((), (), s32[]{:S(2)}) async-start(), calls=%async_computation.1 | async-start | bytes 7833600 | tf_op jit(solution)/shard_map/all_gather | solution.py:44
  7.9 152.9 %all-gather.8.cloned.1.call-start = ((), (), s32[]{:S(2)}) async-start(), calls=%async_computation | async-start | bytes 7833600 | tf_op jit(solution)/shard_map/all_gather | solution.py:43
  8.7 227.0 %all-gather.12.cloned.1.call-start = ((), (), s32[]{:S(2)}) async-start(), calls=%async_computation.2 | async-start | bytes 5570560 | tf_op jit(solution)/shard_map/all_gather | solution.py:60
  171.7 131.6 %all-gather.16.cloned.1.call-start = ((), (), s32[]{:S(2)}) async-start(), calls=%async_computation.4 | async-start | bytes 5744640 | tf_op jit(solution)/shard_map/all_gather | solution.py:118
  172.7 304.2 %all-gather.14.cloned.1.call-start = ((), (), s32[]{:S(2)}) async-start(), calls=%async_computation.3 | async-start | bytes 16015360 | tf_op jit(solution)/shard_map/all_gather | solution.py:10
  303.3 2.6 slice-start
  305.9 3.6 copy-start.7
  305.9 4.2 copy-start.5
  305.9 4.2 copy-start.6
  310.2 12.7 %copy-start.2 = (bf16[4,8,8,640]{3,0,2,1:T(4,128)(2,1)S(1)}, bf16[4,8,8,640]{3,0,2,1:T(4,128)(2,1)}, u32[]{:S(2)}) copy-start(bf16[4,8,8,640]{3,0,2,1:T(4,128)(2,1)} %get-tuple-element.23) | copy-start | bytes 983044
Sparse Core Ops, SparseCore 0:
  10.8 75.4 all-gather.9
  89.2 71.6 all-gather.7
  171.8 63.7 all-gather.11
  238.9 64.4 all-gather.15
  309.6 167.1 all-gather.13
